TPU v7x, 512 devices: a whole 4x4x16 slice. The times are simulated.
512 devices in a mesh: grp: 2 (over core), dp: 32 (over x_hi, z), seq: 8 (over y, x_lo).
Axes of the slice: x: 4 (x_hi: 2, x_lo: 2; x = x_hi * 2 + x_lo), y: 4, z: 16, core: 2. Of those that a mesh axis runs over, the one named last changes fastest.
Arguments:
- latents: float32 [64, 256, 2432], P(('grp', 'dp'), None, 'seq'), may hold values from -6 to 6
- step_noise: bfloat16 [2, 64, 256, 2432], P(None, ('grp', 'dp'), None, 'seq'), may hold values from -6 to 6
- ada_table: float32 [10, 2, 2432], replicated
- qkv_weight: bfloat16 [3, 2048, 2432], P(None, 'seq', ('grp', 'dp')), may hold values from -0.125 to 0.125
- out_weight: bfloat16 [2048, 2432], P(('grp', 'dp'), 'seq'), may hold values from -0.125 to 0.125
- rewards: float32 [64], replicated, may hold values from -4 to 4
- group_ids: int32 [64], replicated, may hold values from 0 to 7, as said below
- time_index: int32 [64], P(('grp', 'dp')), may hold values from 1 to 8
- log_ratio: float32 [2, 64], replicated, may hold values from -0.4 to 0.4
Outputs:
- final_latents: float32 [64, 256, 2432], P(('grp', 'dp'), None, 'seq')
- policy_loss: float32 [], replicated
- out_grad: float32 [2048, 2432], P(('grp', 'dp'), 'seq')
Inputs may be any that keep to these rules, and one draw needn't show every extreme that they name: `group_ids`: each group number names exactly 8 samples.
All inputs are finite; a program needn't handle non-finite values.
Results may differ from a plain program's by a relative error of at most 0.017.
Values may be sent and summed in bfloat16 or wider, within the bound.
No kernel may reach another device: no remote copies, remote signals or barrier semaphores. Data moves between devices by JAX's collectives and lax.ppermute only.
A program may use at most 64 MiB of HBM per device.

v0:
```python
import jax
import jax.numpy as jnp
from jax import lax
from jax.sharding import PartitionSpec as P

HD = 64
TSTEPS = 10
GSIZE = 8
SDE_NOISE = 0.7
CLIP_RANGE = 0.2
REWARD_FLOOR = 0.75
NORM_EPS = 1e-06


def advantages(rewards, group_ids):
    same_group = (group_ids[:, None] == group_ids[None, :]).astype(jnp.float32)
    centre = jnp.sum(same_group * rewards[None, :], 1) / GSIZE
    spread = jnp.sum(same_group * (rewards[None, :] - centre[:, None]) ** 2, 1) / GSIZE
    return (rewards - centre) / jnp.maximum(jnp.sqrt(spread), REWARD_FLOOR)


def policy_terms(advantage, log_ratio):
    ratios = jnp.exp(log_ratio)
    plain = ratios * advantage[None, :]
    bounded = jnp.clip(ratios, 1.0 - CLIP_RANGE, 1.0 + CLIP_RANGE) * advantage[None, :]
    count = 2.0 * advantage.shape[0]
    loss_value = -jnp.sum(jnp.minimum(plain, bounded)) / count
    coef = jnp.where(plain <= bounded, -plain / count, jnp.float32(0.0))
    return (loss_value, coef)


def on_device(
    latents,
    step_noise,
    ada_table,
    qkv_weight,
    out_weight,
    rewards,
    group_ids,
    time_index,
    log_ratio,
):
    qkv_full, out_rows = (
        lax.all_gather(qkv_weight, ("grp", "dp"), axis=2, tiled=True),
        lax.all_gather(out_weight, ("grp", "dp"), axis=0, tiled=True),
    )
    group_width = qkv_full.shape[1]
    heads_here = group_width // HD
    model_width = qkv_full.shape[2]
    projection = qkv_full.reshape(3 * group_width, model_width)
    samples = rewards.shape[0]
    seq_len = latents.shape[1]
    block_rows = min(512, seq_len)
    advantage = advantages(rewards, group_ids)
    loss_value, coef = policy_terms(advantage, log_ratio)
    my_index = lax.axis_index(("grp", "dp"))
    chooser = (jnp.arange(samples, dtype=jnp.int32) == my_index).astype(jnp.float32)
    my_coef = jnp.sum(coef * chooser[None, :], 1)
    step_size = 1.0 / TSTEPS
    state = latents[0]
    attn_list = []
    score_list = []
    plan = jnp.arange(TSTEPS, dtype=jnp.int32)
    for section in range(2):
        index_now = time_index[0] + section
        time_now = 1.0 - index_now.astype(jnp.float32) / TSTEPS
        picker = (plan == index_now).astype(jnp.float32)
        modulate = jnp.sum(picker[:, None, None] * ada_table, 0)
        whole = lax.all_gather(state, "seq", axis=1, tiled=True)
        centre = jnp.mean(whole, -1, keepdims=True)
        spread = jnp.mean((whole - centre) ** 2, -1, keepdims=True)
        normed = (
            (whole - centre) * lax.rsqrt(spread + NORM_EPS) * (1.0 + modulate[0][None, :])
            + modulate[1][None, :]
        ).astype(jnp.bfloat16)
        proj_rows = lax.dot_general(
            normed, projection, (((1,), (1,)), ((), ())), preferred_element_type=jnp.float32
        ).astype(jnp.bfloat16)
        proj_rows = proj_rows.reshape(seq_len, 3, heads_here, HD)
        key_rows = proj_rows[:, 1]
        value_rows = proj_rows[:, 2]
        query_rows = proj_rows[0:block_rows, 0]
        logits = jnp.einsum(
            "qhe,khe->hqk", query_rows, key_rows, preferred_element_type=jnp.float32
        ) * HD ** (-0.5)
        logits = logits - jnp.max(logits, -1, keepdims=True)
        weights = jnp.exp(logits)
        probs = (weights / jnp.sum(weights, -1, keepdims=True)).astype(jnp.bfloat16)
        attn_blocks = jnp.einsum(
            "hqk,khe->qhe", probs, value_rows, preferred_element_type=jnp.float32
        ).astype(jnp.bfloat16)
        attn = attn_blocks.reshape(seq_len, group_width)
        attn_all = lax.all_gather(attn, "seq", axis=1, tiled=True)
        velocity = jnp.dot(attn_all, out_rows, preferred_element_type=jnp.float32)
        noise_level = SDE_NOISE * SDE_NOISE * time_now / (1.0 - time_now)
        std_dev = jnp.sqrt(noise_level * step_size)
        drift = velocity + noise_level / (2.0 * time_now) * (state + (1.0 - time_now) * velocity)
        mean_next = state - step_size * drift
        noise_now = step_noise[section, 0].astype(jnp.float32)
        state = mean_next + std_dev * noise_now
        factor = (
            my_coef[section]
            * -step_size
            * (1.0 + noise_level * (1.0 - time_now) / (2.0 * time_now))
            / std_dev
        )
        score_list.append((factor * noise_now).astype(jnp.bfloat16))
        attn_list.append(attn_all)
    attn_both = jnp.stack(attn_list, 0)
    score_both = jnp.stack(score_list, 0)
    gradient = lax.dot_general(
        attn_both, score_both, (((0, 1), (0, 1)), ((), ())), preferred_element_type=jnp.float32
    )
    out_grad = lax.psum_scatter(gradient, ("grp", "dp"), scatter_dimension=0, tiled=True)
    return (state[None], loss_value, out_grad)


def solution(mesh):
    return jax.shard_map(
        on_device,
        mesh=mesh,
        in_specs=(
            P(("grp", "dp"), None, "seq"),
            P(None, ("grp", "dp"), None, "seq"),
            P(),
            P(None, "seq", ("grp", "dp")),
            P(("grp", "dp"), "seq"),
            P(),
            P(),
            P(("grp", "dp")),
            P(),
        ),
        out_specs=(P(("grp", "dp"), None, "seq"), P(), P(("grp", "dp"), "seq")),
        check_vma=False,
    )
```

profile of v0, /device:TPU:8, one launch (start us, length us, event | category | flops | bytes accessed | tf_op | source)
XLA Modules:
  0.0 781.1 jit_solution(5501011536457915289)
XLA Ops:
  7.2 0.0 all-gather.18.cloned.1.call-start
  7.2 0.7 all-gather.18.cloned.1.call-update
  7.9 0.0 all-gather.8.cloned.1.call-start
  7.9 1.5 copy.31
  9.4 0.0 all-gather.8.cloned.1.call-update
  9.5 0.0 all-gather.12.cloned.1.call-start
  9.5 0.7 all-gather.12.cloned.1.call-update
  10.2 0.0 all-gather.10.cloned.1.call-start
  10.9 1.2 multiply_reduce_fusion.2
  12.1 0.1 fusion.35
  12.2 67.8 %all-gather.18.cloned.1.call-done = f32[1,256,2432]{1,2,0:T(8,128)} async-done(((f32[1,256,304]{1,2,0:T(8,128)}), f32[1,256,2432]{1,2,0:T(8,128)}) %all-gather.18.cloned.1.call-update) | async-done | bytes 2490384 | tf_op jit(solution)/shard_map/all_gather | solution.py:69
  79.9 2.2 reduce_sum.108
  82.1 0.3 copy-done
  82.4 0.4 multiply_reduce_fusion.1
  82.7 155.8 %all-gather.8.cloned.1.call-done = bf16[3,256,2432]{1,0,2:T(4,128)(2,1)} async-done(((bf16[3,256,38]{1,0,2:T(4,128)(2,1)}), bf16[3,256,2432]{1,0,2:T(4,128)(2,1)}) %all-gather.8.cloned.1.call-update) | async-done | bytes 3735568 | tf_op jit(solution)/shard_map/all_gather | solution.py:44
  238.6 8.5 %copy.32 = bf16[3,256,2432]{2,1,0:T(8,128)(2,1)} copy(bf16[3,256,2432]{1,0,2:T(4,128)(2,1)} %all-gather.8.cloned.1.call-done) | data formatting | bytes 7471104 | tf_op jit(solution)/shard_map/all_gather | solution.py:44
  247.1 4.0 convolution_convert_fusion.1
  251.2 0.2 copy.33
  251.4 0.5 fusion.44
  251.9 0.3 convolution_multiply_fusion.1
  252.3 1.0 convolution_convert_fusion.3
  253.3 0.0 all-gather.14.cloned.1.call-start
  253.5 124.9 %all-gather.12.cloned.1.call-done = bf16[2048,304]{1,0:T(8,128)(2,1)} async-done(((bf16[32,304]{1,0:T(8,128)(2,1)}), bf16[2048,304]{1,0:T(8,128)(2,1)}) %all-gather.12.cloned.1.call-update) | async-done | bytes 1245200 | tf_op jit(solution)/shard_map/all_gather | solution.py:45
  378.4 43.7 %all-gather.10.cloned.1.call-done = bf16[256,2048]{0,1:T(8,128)(2,1)} async-done(((bf16[256,256]{0,1:T(8,128)(2,1)}), bf16[256,2048]{0,1:T(8,128)(2,1)}) %all-gather.10.cloned.1.call-update) | async-done | bytes 1048592 | tf_op jit(solution)/shard_map/all_gather | solution.py:93
  422.1 3.1 fusion.18
  425.3 0.0 all-gather.16.cloned.1.call-start
  425.4 0.1 fusion.34
  425.4 66.3 %all-gather.14.cloned.1.call-done = f32[256,2432]{0,1:T(8,128)} async-done(((f32[256,304]{0,1:T(8,128)}), f32[256,2432]{0,1:T(8,128)}) %all-gather.14.cloned.1.call-update) | async-done | bytes 2490384 | tf_op jit(solution)/shard_map/all_gather | solution.py:69
  491.8 2.2 reduce_sum.112
  494.0 0.3 copy-done.1
  494.2 0.4 multiply_reduce_fusion
  494.6 4.0 convolution_convert_fusion
  498.6 0.2 copy.35
  498.8 0.5 fusion.45
  499.3 0.3 convolution_multiply_fusion
  499.7 1.0 convolution_convert_fusion.2
  500.8 0.0 reduce-scatter.2.cloned.1.call-start
  501.0 0.2 fusion.32
  501.2 0.2 fusion.33
  501.4 0.7 fusion.37
  502.1 0.6 fusion.43
  504.0 0.1 fusion.31
  504.1 44.7 %all-gather.16.cloned.1.call-done = bf16[256,2048]{0,1:T(8,128)(2,1)} async-done(((bf16[256,256]{0,1:T(8,128)(2,1)}), bf16[256,2048]{0,1:T(8,128)(2,1)}) %all-gather.16.cloned.1.call-update) | async-done | bytes 1048592 | tf_op jit(solution)/shard_map/all_gather | solution.py:93
  548.8 4.2 convolution_bitcast_fusion
  553.8 0.1 copy-done.4
  553.9 0.6 copy-done.8
  554.5 2.6 fusion.22
  557.1 215.9 %reduce-scatter.2.cloned.1.call-done = f32[32,304]{1,0:T(8,128)} async-done(((f32[2048,304]{1,0:T(8,128)}), f32[32,304]{1,0:T(8,128)}) %reduce-scatter.2.cloned.1.call-update) | async-done | bytes 38928 | tf_op jit(solution)/shard_map/reduce_scatter | solution.py:114
  (28 shorter events, 0.2 us)
Async XLA Ops:
  7.2 72.8 %all-gather.18.cloned.1.call-start = ((), (), s32[]{:S(2)}) async-start(), calls=%async_computation.7 | async-start | bytes 2801664 | tf_op jit(solution)/shard_map/all_gather | solution.py:69
  7.9 230.7 %all-gather.8.cloned.1.call-start = ((), (), s32[]{:S(2)}) async-start(), calls=%async_computation.1 | async-start | bytes 5058560 | tf_op jit(solution)/shard_map/all_gather | solution.py:44
  9.5 369.0 %all-gather.12.cloned.1.call-start = ((), (), s32[]{:S(2)}) async-start(), calls=%async_computation.3 | async-start | bytes 1597440 | tf_op jit(solution)/shard_map/all_gather | solution.py:45
  10.2 411.9 %all-gather.10.cloned.1.call-start = ((), (), s32[]{:S(2)}) async-start(), calls=%async_computation.2 | async-start | bytes 1179648 | tf_op jit(solution)/shard_map/all_gather | solution.py:93
  79.9 2.5 copy-start
  252.2 169.9 %copy-start.2 = (f32[1,256,304]{1,2,0:T(8,128)S(1)}, f32[1,256,304]{1,2,0:T(8,128)}, u32[]{:S(2)}) copy-start(f32[1,256,304]{1,2,0:T(8,128)} %param.9) | copy-start | bytes 933892
  252.2 169.9 %copy-start.3 = (bf16[2,1,256,304]{2,3,1,0:T(8,128)(2,1)S(1)}, bf16[2,1,256,304]{2,3,1,0:T(8,128)(2,1)}, u32[]{:S(2)}) copy-start(bf16[2,1,256,304]{2,3,1,0:T(8,128)(2,1)} %param.10) | copy-start | bytes 933892
  253.3 238.4 %all-gather.14.cloned.1.call-start = ((), (), s32[]{:S(2)}) async-start(), calls=%async_computation.4 | async-start | bytes 2801664 | tf_op jit(solution)/shard_map/all_gather | solution.py:69
  425.3 123.5 %all-gather.16.cloned.1.call-start = ((), (), s32[]{:S(2)}) async-start(), calls=%async_computation.5 | async-start | bytes 1179648 | tf_op jit(solution)/shard_map/all_gather | solution.py:93
  491.8 2.5 copy-start.1
  499.7 1.3 copy-start.5
  499.7 1.3 copy-start.6
  499.7 1.7 copy-start.7
  499.7 49.1 %copy-start.9 = (bf16[256,2048]{0,1:T(8,128)(2,1)S(1)}, bf16[256,2048]{0,1:T(8,128)(2,1)}, u32[]{:S(2)}) copy-start(bf16[256,2048]{0,1:T(8,128)(2,1)} %all-gather.10.cloned.1.call-done) | copy-start | bytes 3145732
  500.8 272.3 %reduce-scatter.2.cloned.1.call-start = ((), (), s32[]{:S(2)}) async-start(), calls=%async_computation.6 | async-start | bytes 3194880 | tf_op jit(solution)/shard_map/reduce_scatter | solution.py:114
  553.0 1.0 copy-start.4
  553.0 1.5 copy-start.8
Sparse Core Ops, SparseCore 0:
  10.1 69.8 all-gather.17
  83.7 154.8 all-gather.7
  241.9 136.5 all-gather.11
  380.9 41.1 all-gather.9
  425.4 66.2 all-gather.13
  500.9 47.8 all-gather.15
  554.1 218.9 reduce-scatter.1
where the time goes:
time: 782 us; the launch traced here: 781 us
  waiting for transfers between devices  721 us (92%)
  matrix products  21.8 us (3%)
  between operations  18.5 us (2%)
  local copies, waits for them, and re-layouts  12.2 us (2%)
    reduce_scatter x1, waiting for transfers between devices, on_device(): lax.psum_scatter(gradient, ('grp', 'dp'), scatter_dimension=0, tiled=True)  216 us
    all_gather x1, waiting for transfers between devices, on_device(): lax.all_gather(qkv_weight, ('grp', 'dp'), axis=2, tiled=True)  156 us
    all_gather x2, waiting for transfers between devices, on_device(): whole = lax.all_gather(state, 'seq', axis=1, tiled=True)  134 us
    all_gather x1, waiting for transfers between devices, on_device(): lax.all_gather(out_weight, ('grp', 'dp'), axis=0, tiled=True)  125 us
    all_gather x2, waiting for transfers between devices, on_device(): attn_all = lax.all_gather(attn, 'seq', axis=1, tiled=True)  88.4 us
  transfers between devices with their start and end apart: 7, of which 7 were waited for; matrix products, arithmetic and copies ran while one was open for 3% of the time, Pallas kernels for 0%

commit v1 on v0

--- a/solution.py
+++ b/solution.py
@@ -41,7 +41,12 @@
     log_ratio,
 ):
     qkv_full, out_rows = (
-        lax.all_gather(qkv_weight, ("grp", "dp"), axis=2, tiled=True),
+        jnp.concatenate(
+            lax.all_to_all(
+                jnp.stack([qkv_weight] * lax.axis_size(("grp", "dp"))), ("grp", "dp"), 0, 0
+            ),
+            axis=2,
+        ),
         lax.all_gather(out_weight, ("grp", "dp"), axis=0, tiled=True),
     )
     group_width = qkv_full.shape[1]

time: 782 us -> 691 us (0.88)
  waiting for transfers between devices: 721 us -> 614 us
  starting transfers between devices: 0.28 us -> 19.3 us
    all_gather x1 -> x0, waiting for transfers between devices: 156 us -> none  [on_device(): lax.all_gather(qkv_weight, ('grp', 'dp'), axis=2, tiled=True)]
    all_to_all x0 -> x1, waiting for transfers between devices: none -> 92.5 us  [on_device(): lax.all_to_all(jnp.stack([qkv_weight] * lax.axis_size(('grp', 'dp'))), ('...]
    all_gather x1, waiting for transfers between devices: 125 us -> 69.1 us  [on_device(): lax.all_gather(out_weight, ('grp', 'dp'), axis=0, tiled=True)]
    all_to_all x0 -> x1, starting transfers between devices: none -> 18.9 us  [on_device(): lax.all_to_all(jnp.stack([qkv_weight] * lax.axis_size(('grp', 'dp'))), ('...]
    all_gather x2, waiting for transfers between devices: 134 us -> 147 us  [on_device(): whole = lax.all_gather(state, 'seq', axis=1, tiled=True)]
    all_gather x1 -> x0, local copies, waits for them, and re-layouts: 8.55 us -> none  [on_device(): lax.all_gather(qkv_weight, ('grp', 'dp'), axis=2, tiled=True)]
  transfers between devices with their start and end apart: 7 -> 7, of which waited for: 7 -> 7; matrix products, arithmetic and copies ran while one was open for 3% -> 2% of each run, Pallas kernels for 0% -> 0%
where the time goes in v1:
time: 691 us; the launch traced here: 690 us
  waiting for transfers between devices  614 us (89%)
  starting transfers between devices  19.3 us (3%)
  matrix products  19.3 us (3%)
  between operations  18.6 us (3%)
  local copies, waits for them, and re-layouts  12.1 us (2%)
    reduce_scatter x1, waiting for transfers between devices, on_device(): lax.psum_scatter(gradient, ('grp', 'dp'), scatter_dimension=0, tiled=True)  216 us
    all_gather x2, waiting for transfers between devices, on_device(): whole = lax.all_gather(state, 'seq', axis=1, tiled=True)  147 us
    all_to_all x1, waiting for transfers between devices, on_device(): lax.all_to_all(jnp.stack([qkv_weight] * lax.axis_size(('grp', 'dp'))), ('...  92.5 us
    all_gather x2, waiting for transfers between devices, on_device(): attn_all = lax.all_gather(attn, 'seq', axis=1, tiled=True)  88.5 us
    all_gather x1, waiting for transfers between devices, on_device(): lax.all_gather(out_weight, ('grp', 'dp'), axis=0, tiled=True)  69.1 us
    all_to_all x1, starting transfers between devices, on_device(): lax.all_to_all(jnp.stack([qkv_weight] * lax.axis_size(('grp', 'dp'))), ('...  18.9 us
  transfers between devices with their start and end apart: 7, of which 7 were waited for; matrix products, arithmetic and copies ran while one was open for 2% of the time, Pallas kernels for 0%

profile of v1, /device:TPU:8, one launch (start us, length us, event | category | flops | bytes accessed | tf_op | source)
XLA Modules:
  0.0 690.1 jit_solution(9904969713829516201)
XLA Ops:
  7.2 3.0 stack.10
  10.1 18.9 %all-to-all-start = ((bf16[64,3,256,38]{2,3,1,0:T(8,128)(2,1)}), bf16[64,3,256,38]{2,3,1,0:T(8,128)(2,1)}, u32[]{:S(2)}, u32[]{:S(2)}) async-start(bf16[64,3,256,38]{2,3,1,0:T(8,128)(2,1)} %stack.10), calls=%async_computation | async-start | bytes 7864320 | tf_op jit(solution)/shard_map/all_to_all | solution.py:45
  29.1 0.0 all-gather.15.cloned.1.call-start
  29.1 0.7 all-gather.15.cloned.1.call-update
  29.9 0.7 all-gather.9.cloned.1.call-update
  30.6 0.0 all-gather.7.cloned.1.call-start
  31.3 0.2 multiply_reduce_fusion.2
  31.5 0.1 fusion.35
  31.6 80.7 %all-gather.15.cloned.1.call-done = f32[1,256,2432]{1,2,0:T(8,128)} async-done(((f32[1,256,304]{1,2,0:T(8,128)}), f32[1,256,2432]{1,2,0:T(8,128)}) %all-gather.15.cloned.1.call-update) | async-done | bytes 2490384 | tf_op jit(solution)/shard_map/all_gather | solution.py:74
  112.3 2.2 reduce_sum.108
  114.4 0.3 copy-done
  114.7 0.4 multiply_reduce_fusion.1
  115.1 92.5 %all-to-all-done = bf16[64,3,256,38]{2,3,1,0:T(8,128)(2,1)} async-done(((bf16[64,3,256,38]{2,3,1,0:T(8,128)(2,1)}), bf16[64,3,256,38]{2,3,1,0:T(8,128)(2,1)}, u32[]{:S(2)}, u32[]{:S(2)}) %all-to-all-start) | async-done | bytes 3735584 | tf_op jit(solution)/shard_map/all_to_all | solution.py:45
  207.6 4.0 copy.31
  211.6 1.1 copy.38
  212.7 1.8 copy-done.2
  214.5 1.8 convolution_convert_fusion.1
  216.3 0.2 copy.32
  216.5 0.5 fusion.44
  217.0 0.3 convolution_multiply_fusion.1
  217.4 1.0 convolution_convert_fusion.3
  218.5 0.0 all-gather.11.cloned.1.call-start
  218.7 69.1 %all-gather.9.cloned.1.call-done = bf16[2048,304]{1,0:T(8,128)(2,1)} async-done(((bf16[32,304]{1,0:T(8,128)(2,1)}), bf16[2048,304]{1,0:T(8,128)(2,1)}) %all-gather.9.cloned.1.call-update) | async-done | bytes 1245200 | tf_op jit(solution)/shard_map/all_gather | solution.py:50
  287.7 43.9 %all-gather.7.cloned.1.call-done = bf16[256,2048]{0,1:T(8,128)(2,1)} async-done(((bf16[256,256]{0,1:T(8,128)(2,1)}), bf16[256,2048]{0,1:T(8,128)(2,1)}) %all-gather.7.cloned.1.call-update) | async-done | bytes 1048592 | tf_op jit(solution)/shard_map/all_gather | solution.py:98
  331.6 3.1 fusion.18
  334.8 0.2 all-gather.13.cloned.1.call-start
  335.0 0.1 fusion.34
  335.0 66.2 %all-gather.11.cloned.1.call-done = f32[256,2432]{0,1:T(8,128)} async-done(((f32[256,304]{0,1:T(8,128)}), f32[256,2432]{0,1:T(8,128)}) %all-gather.11.cloned.1.call-update) | async-done | bytes 2490384 | tf_op jit(solution)/shard_map/all_gather | solution.py:74
  401.2 2.2 reduce_sum.112
  403.4 0.3 copy-done.1
  403.7 0.4 multiply_reduce_fusion
  404.0 3.8 convolution_convert_fusion
  407.8 0.2 copy.34
  408.0 0.5 fusion.45
  408.5 0.3 convolution_multiply_fusion
  408.9 1.0 convolution_convert_fusion.2
  410.0 0.0 reduce-scatter.2.cloned.1.call-start
  410.2 0.2 fusion.32
  410.4 0.2 fusion.33
  410.6 0.7 fusion.37
  411.3 0.6 fusion.43
  413.3 0.1 fusion.31
  413.3 44.7 %all-gather.13.cloned.1.call-done = bf16[256,2048]{0,1:T(8,128)(2,1)} async-done(((bf16[256,256]{0,1:T(8,128)(2,1)}), bf16[256,2048]{0,1:T(8,128)(2,1)}) %all-gather.13.cloned.1.call-update) | async-done | bytes 1048592 | tf_op jit(solution)/shard_map/all_gather | solution.py:98
  458.0 4.2 convolution_bitcast_fusion
  463.0 0.1 copy-done.5
  463.1 0.6 copy-done.10
  463.7 2.6 fusion.22
  466.3 215.8 %reduce-scatter.2.cloned.1.call-done = f32[32,304]{1,0:T(8,128)} async-done(((f32[2048,304]{1,0:T(8,128)}), f32[32,304]{1,0:T(8,128)}) %reduce-scatter.2.cloned.1.call-update) | async-done | bytes 38928 | tf_op jit(solution)/shard_map/reduce_scatter | solution.py:119
  (32 shorter events, 0.2 us)
Async XLA Ops:
  10.1 21.1 %copy-start.6 = (f32[10,2,2432]{2,1,0:T(2,128)S(1)}, f32[10,2,2432]{2,1,0:T(2,128)}, u32[]{:S(2)}) copy-start(f32[10,2,2432]{2,1,0:T(2,128)} %param.11) | copy-start | bytes 583684
  10.1 197.4 %all-to-all-start = ((bf16[64,3,256,38]{2,3,1,0:T(8,128)(2,1)}), bf16[64,3,256,38]{2,3,1,0:T(8,128)(2,1)}, u32[]{:S(2)}, u32[]{:S(2)}) async-start(bf16[64,3,256,38]{2,3,1,0:T(8,128)(2,1)} %stack.10), calls=%async_computation | async-start | bytes 7864320 | tf_op jit(solution)/shard_map/all_to_all | solution.py:45
  29.1 83.2 %all-gather.15.cloned.1.call-start = ((), (), s32[]{:S(2)}) async-start(), calls=%async_computation.7 | async-start | bytes 2801664 | tf_op jit(solution)/shard_map/all_gather | solution.py:74
  29.8 257.9 %all-gather.9.cloned.1.call-start = ((), (), s32[]{:S(2)}) async-start(), calls=%async_computation.3 | async-start | bytes 1597440 | tf_op jit(solution)/shard_map/all_gather | solution.py:50
  30.6 301.0 %all-gather.7.cloned.1.call-start = ((), (), s32[]{:S(2)}) async-start(), calls=%async_computation.2 | async-start | bytes 1179648 | tf_op jit(solution)/shard_map/all_gather | solution.py:98
  112.3 2.5 copy-start
  212.7 1.8 copy-start.2
  217.4 114.2 %copy-start.3 = (f32[1,256,304]{1,2,0:T(8,128)S(1)}, f32[1,256,304]{1,2,0:T(8,128)}, u32[]{:S(2)}) copy-start(f32[1,256,304]{1,2,0:T(8,128)} %param.9) | copy-start | bytes 933892
  217.4 114.2 %copy-start.4 = (bf16[2,1,256,304]{2,3,1,0:T(8,128)(2,1)S(1)}, bf16[2,1,256,304]{2,3,1,0:T(8,128)(2,1)}, u32[]{:S(2)}) copy-start(bf16[2,1,256,304]{2,3,1,0:T(8,128)(2,1)} %param.10) | copy-start | bytes 933892
  218.5 182.7 %all-gather.11.cloned.1.call-start = ((), (), s32[]{:S(2)}) async-start(), calls=%async_computation.4 | async-start | bytes 2801664 | tf_op jit(solution)/shard_map/all_gather | solution.py:74
  334.8 123.2 %all-gather.13.cloned.1.call-start = ((), (), s32[]{:S(2)}) async-start(), calls=%async_computation.5 | async-start | bytes 1179648 | tf_op jit(solution)/shard_map/all_gather | solution.py:98
  401.2 2.5 copy-start.1
  408.9 1.3 copy-start.7
  408.9 1.3 copy-start.8
  408.9 1.7 copy-start.9
  408.9 49.1 %copy-start.11 = (bf16[256,2048]{0,1:T(8,128)(2,1)S(1)}, bf16[256,2048]{0,1:T(8,128)(2,1)}, u32[]{:S(2)}) copy-start(bf16[256,2048]{0,1:T(8,128)(2,1)} %all-gather.7.cloned.1.call-done) | copy-start | bytes 3145732
  410.0 272.1 %reduce-scatter.2.cloned.1.call-start = ((), (), s32[]{:S(2)}) async-start(), calls=%async_computation.6 | async-start | bytes 3194880 | tf_op jit(solution)/shard_map/reduce_scatter | solution.py:119
  462.1 1.0 copy-start.5
  462.2 1.5 copy-start.10
Sparse Core Ops, SparseCore 0:
  32.0 80.2 all-gather.14
  115.5 172.1 all-gather.8
  290.4 41.1 all-gather.6
  334.9 66.2 all-gather.10
  410.1 47.8 all-gather.12
  463.1 218.9 reduce-scatter.1
